TPU v7x, 32 devices: a whole 2x2x4 slice. The times are simulated.
32 devices in a mesh: dp: 8 (over z, y), ctx: 4 (over x, core).
Axes of the slice: x: 2, y: 2, z: 4, core: 2. Of those that a mesh axis runs over, the one named last changes fastest.
Arguments:
- queries: bfloat16 [4096, 4096], P(('dp', 'ctx')), may hold values from -40 to 40
- key_head_inputs: bfloat16 [4096, 512], P(('dp', 'ctx')), may hold values from -40 to 40
- value_head_inputs: bfloat16 [4096, 512], P(('dp', 'ctx')), may hold values from -6 to 6
- output_gradient: bfloat16 [4096, 4096], P(('dp', 'ctx')), may hold values from -6 to 6
- positions: int32 [4096], P(('dp', 'ctx')), may hold values from 0 to 1023, as said below
- counts: int32 [32], P(('dp', 'ctx')), may hold values from 64 to 128, as said below
- inputs: bfloat16 [4096, 8192], P(('dp', 'ctx')), may hold values from -6 to 6
Outputs:
- query_grad: bfloat16 [4096, 4096], P(('dp', 'ctx'))
- key_grad: bfloat16 [4096, 512], P(('dp', 'ctx'))
- value_grad: bfloat16 [4096, 512], P(('dp', 'ctx'))
- value_weight_gradient: float32 [512, 8192], P('dp', 'ctx')
Inputs may be any that keep to these rules, and one draw needn't show every extreme that they name: A device's valid slots are its first counts slots; the others are padding. Some device holds 128 valid slots. Along a sequence the positions of valid slots rise strictly; the first slot holds 0 and the last valid slot 1023. A padding slot repeats the position before it, or holds 1023 after the last valid slot.
All inputs are finite; a program needn't handle non-finite values.
Results may differ from a plain program's by a relative error of at most 0.0061.
Values may be sent and summed in bfloat16 or wider, within the bound.
No kernel may reach another device: no remote copies, remote signals or barrier semaphores. Data moves between devices by JAX's collectives and lax.ppermute only.
A program may use at most 128 MiB of HBM per device.

v0:
```python
import math

import jax
import jax.numpy as jnp
from jax import lax
from jax.sharding import PartitionSpec as P

HEAD_DIM = 128
QUERY_HEADS = 32
KEY_HEADS = 4


THETA = 500000.0


def rope_tables(position, head_size):
    half_width = head_size // 2
    frequency = jnp.exp(
        jnp.arange(half_width, dtype=jnp.float32) * (-2.0 * math.log(THETA) / head_size)
    )
    angles = position.astype(jnp.float32)[:, None] * frequency[None, :]
    return (jnp.cos(angles), jnp.sin(angles))


def apply_rotation(vectors, cosine_table, sine_lookup, sense):
    half_width = vectors.shape[-1] // 2
    lower_half = vectors[..., :half_width]
    upper_half = vectors[..., half_width:]
    cos_part = cosine_table[:, None, :]
    sin_part = sine_lookup[:, None, :] * sense
    return jnp.concatenate(
        [
            lower_half * cos_part - upper_half * sin_part,
            upper_half * cos_part + lower_half * sin_part,
        ],
        axis=-1,
    )


def per_device(
    queries, key_head_inputs, value_head_inputs, output_gradient, positions, counts, inputs
):
    row_number_total = queries.shape[0]
    query_group_width = QUERY_HEADS // KEY_HEADS
    axis_span = lax.axis_size("ctx")
    retained_slots = row_number_total * axis_span
    key_block = min(512, retained_slots)
    my_index = lax.axis_index("ctx")
    score_scale = 1.0 / math.sqrt(HEAD_DIM)
    cosine_table, sine_lookup = rope_tables(positions, HEAD_DIM)
    query_rotated = apply_rotation(
        queries.reshape(row_number_total, QUERY_HEADS, HEAD_DIM).astype(jnp.float32),
        cosine_table,
        sine_lookup,
        1.0,
    ).astype(jnp.bfloat16)
    key_rotated = apply_rotation(
        key_head_inputs.reshape(row_number_total, KEY_HEADS, HEAD_DIM).astype(jnp.float32),
        cosine_table,
        sine_lookup,
        1.0,
    ).astype(jnp.bfloat16)
    key_rotated = key_rotated.reshape(row_number_total, KEY_HEADS * HEAD_DIM)
    key_row_block, value_row_block, all_counts = (
        lax.all_gather(key_rotated, "ctx", axis=0, tiled=True),
        lax.all_gather(value_head_inputs, "ctx", axis=0, tiled=True),
        lax.all_gather(counts, "ctx", axis=0, tiled=True),
    )
    gathered_keys = key_row_block.reshape(retained_slots, KEY_HEADS, HEAD_DIM)
    gathered_values = value_row_block.reshape(retained_slots, KEY_HEADS, HEAD_DIM)
    key_valid = jnp.arange(retained_slots, dtype=jnp.int32) % row_number_total < jnp.repeat(
        all_counts, row_number_total
    )
    own_valid = jnp.arange(row_number_total, dtype=jnp.int32) < counts[0]
    initial_gradients = jnp.zeros((retained_slots, KEY_HEADS, HEAD_DIM), jnp.float32)
    first_slot = my_index * row_number_total
    key_accumulator = initial_gradients
    value_accumulator = initial_gradients
    query_count = query_rotated.shape[0]
    query_grouped = query_rotated.reshape(query_count, KEY_HEADS, query_group_width, HEAD_DIM)
    output_grad_grouped = output_gradient.reshape(
        query_count, KEY_HEADS, query_group_width, HEAD_DIM
    )
    q_slots = first_slot + jnp.arange(query_count, dtype=jnp.int32)
    block_total = (first_slot + query_count - 1) // key_block + 1

    def scores_for(begin_at):
        k_blk = lax.dynamic_slice_in_dim(gathered_keys, begin_at, key_block, 0)
        v_blk = lax.dynamic_slice_in_dim(gathered_values, begin_at, key_block, 0)
        k_slots = begin_at + jnp.arange(key_block, dtype=jnp.int32)
        k_valid = lax.dynamic_slice_in_dim(key_valid, begin_at, key_block, 0)
        allowed = own_valid[:, None] & k_valid[None, :] & (k_slots[None, :] <= q_slots[:, None])
        scores = (
            jnp.einsum("qhgd,khd->hgqk", query_grouped, k_blk, preferred_element_type=jnp.float32)
            * score_scale
        )
        d_probs = jnp.einsum(
            "qhgd,khd->hgqk", output_grad_grouped, v_blk, preferred_element_type=jnp.float32
        )
        return (k_blk, scores, d_probs, allowed)

    def first_pass(step_index, carry):
        row_top, row_total, weighted = carry
        k_blk, scores, d_probs, allowed = scores_for(step_index * key_block)
        new_top = jnp.maximum(row_top, jnp.max(jnp.where(allowed, scores, -1e30), axis=-1))
        factor = jnp.exp(row_top - new_top)
        exp_terms = jnp.where(allowed, jnp.exp(scores - new_top[..., None]), 0.0)
        return (
            new_top,
            row_total * factor + jnp.sum(exp_terms, axis=-1),
            weighted * factor + jnp.sum(exp_terms * d_probs, axis=-1),
        )

    statistic_shape = (KEY_HEADS, query_group_width, query_count)
    start_stats = (
        jnp.full(statistic_shape, -1e30, jnp.float32),
        jnp.zeros(statistic_shape, jnp.float32),
        jnp.zeros(statistic_shape, jnp.float32),
    )
    row_top, row_total, weighted = lax.fori_loop(0, block_total, first_pass, start_stats)
    row_total = jnp.where(own_valid[None, None, :], row_total, 1.0)
    row_delta = weighted / row_total

    def second_pass(step_index, carry):
        q_acc, key_sum, value_sum = carry
        begin_at = step_index * key_block
        k_blk, scores, d_probs, allowed = scores_for(begin_at)
        softmax = (
            jnp.where(allowed, jnp.exp(scores - row_top[..., None]), 0.0) / row_total[..., None]
        )
        d_scores = softmax * (d_probs - row_delta[..., None]) * score_scale
        prob_bf = softmax.astype(jnp.bfloat16)
        dscore_bf = d_scores.astype(jnp.bfloat16)
        q_acc = q_acc + jnp.einsum(
            "hgqk,khd->qhgd", dscore_bf, k_blk, preferred_element_type=jnp.float32
        )
        k_piece = jnp.einsum(
            "hgqk,qhgd->khd", dscore_bf, query_grouped, preferred_element_type=jnp.float32
        )
        v_piece = jnp.einsum(
            "hgqk,qhgd->khd", prob_bf, output_grad_grouped, preferred_element_type=jnp.float32
        )
        key_sum = lax.dynamic_update_slice_in_dim(
            key_sum,
            lax.dynamic_slice_in_dim(key_sum, begin_at, key_block, 0) + k_piece,
            begin_at,
            0,
        )
        value_sum = lax.dynamic_update_slice_in_dim(
            value_sum,
            lax.dynamic_slice_in_dim(value_sum, begin_at, key_block, 0) + v_piece,
            begin_at,
            0,
        )
        return (q_acc, key_sum, value_sum)

    query_offset = jnp.zeros((query_count, KEY_HEADS, query_group_width, HEAD_DIM), jnp.float32)
    q_acc, key_accumulator, value_accumulator = lax.fori_loop(
        0, block_total, second_pass, (query_offset, key_accumulator, value_accumulator)
    )
    q_grad_rot, key_accumulator, value_accumulator = (
        q_acc.reshape(query_count, QUERY_HEADS, HEAD_DIM),
        key_accumulator,
        value_accumulator,
    )
    key_portion, value_part = (
        lax.psum_scatter(
            key_accumulator.reshape(retained_slots, KEY_HEADS * HEAD_DIM),
            "ctx",
            scatter_dimension=0,
            tiled=True,
        ),
        lax.psum_scatter(
            value_accumulator.reshape(retained_slots, KEY_HEADS * HEAD_DIM),
            "ctx",
            scatter_dimension=0,
            tiled=True,
        ),
    )
    query_grad = (
        apply_rotation(q_grad_rot, cosine_table, sine_lookup, -1.0)
        .astype(jnp.bfloat16)
        .reshape(row_number_total, QUERY_HEADS * HEAD_DIM)
    )
    key_grad = (
        apply_rotation(
            key_portion.reshape(row_number_total, KEY_HEADS, HEAD_DIM),
            cosine_table,
            sine_lookup,
            -1.0,
        )
        .astype(jnp.bfloat16)
        .reshape(row_number_total, KEY_HEADS * HEAD_DIM)
    )
    value_grad = value_part.astype(jnp.bfloat16)
    weight_part = lax.psum_scatter(
        lax.dot_general(
            inputs, value_grad, (((0,), (0,)), ((), ())), preferred_element_type=jnp.float32
        ),
        "ctx",
        scatter_dimension=0,
        tiled=True,
    )
    shares = lax.psum_scatter(weight_part, "dp", scatter_dimension=1, tiled=True)
    return (query_grad, key_grad, value_grad, shares.T)


def solution(mesh):
    placed = (
        P(("dp", "ctx"), None),
        P(("dp", "ctx"), None),
        P(("dp", "ctx"), None),
        P(("dp", "ctx"), None),
        P(("dp", "ctx")),
        P(("dp", "ctx")),
        P(("dp", "ctx"), None),
    )
    return jax.shard_map(
        per_device,
        mesh=mesh,
        in_specs=placed,
        out_specs=(
            P(("dp", "ctx"), None),
            P(("dp", "ctx"), None),
            P(("dp", "ctx"), None),
            P("dp", "ctx"),
        ),
        check_vma=False,
    )
```

profile of v0, /device:TPU:0, one launch (start us, length us, event | category | flops | bytes accessed | tf_op | source)
XLA Modules:
  0.0 355.9 jit_solution(10259633255239488766)
XLA Ops:
  8.1 1.2 dynamic-slice
  9.3 0.8 dynamic-update-slice
  10.1 0.7 convert_element_type.43
  10.7 6.4 %all-reduce = s32[4]{0:T(128)S(1)} all-reduce(s32[4]{0:T(128)S(1)} %dynamic-update-slice), channel_id=1, replica_groups=mesh['dp'=8,'ctx'=4] {'ctx'}, use_global_device_ids=true, to_apply=%add | all-reduce | flops 4 | bytes 32
  17.1 0.8 broadcast_multiply_fusion
  18.1 1.0 copy.24
  19.1 1.0 copy.46
  20.2 6.6 %all_gather.10 = bf16[512,512]{0,1:T(8,128)(2,1)S(1)} all-gather(bf16[128,512]{0,1:T(8,128)(2,1)S(1)} %bitcast.175), channel_id=1, replica_groups=mesh['dp'=8,'ctx'=4] {'ctx'}, dimensions={0}, use_global_device_ids=true | all-gather | bytes 655360 | tf_op jit(solution)/shard_map/all_gather | solution.py:65
  26.8 1.0 copy.29
  27.8 7.3 %all_gather.11 = bf16[512,512]{0,1:T(8,128)(2,1)S(1)} all-gather(bf16[128,512]{0,1:T(8,128)(2,1)S(1)} %copy.24), channel_id=1, replica_groups=mesh['dp'=8,'ctx'=4] {'ctx'}, dimensions={0}, use_global_device_ids=true | all-gather | bytes 655360 | tf_op jit(solution)/shard_map/all_gather | solution.py:66
  35.1 1.0 copy.27
  36.1 1.6 copy.25
  37.7 1.3 copy.28
  39.1 1.4 convert_bitcast_fusion
  40.9 0.8 subtract_convert_fusion.1
  42.1 0.4 copy.23
  42.5 0.6 pad_maximum_fusion
  43.1 7.6 %while.30 = (s32[]{:T(128)}, f32[4,8,128]{2,1,0:T(8,128)S(1)}, f32[4,8,128]{2,1,0:T(8,128)S(1)}, f32[4,8,128]{2,1,0:T(8,128)S(1)}, s32[]{:T(128)}, /*index=5*/bf...) while((s32[]{:T(128)}, f32[4,8,128]{2,1,0:T(8,128)S(1)}, ...), condition=%wide.region_4.5_spmd.clone, body=%wide.region_0.4_spmd.clone.sunk | while | flops 1099120896 | bytes 35166692 | solution.py:120
  43.2 0.6 iota_compare_fusion.5
  44.1 2.3 fusion.85
  46.5 1.8 fusion.87
  48.3 2.4 fusion.86
  50.8 1.1 broadcast_in_dim.66.clone
  51.8 1.0 broadcast_in_dim.66
  52.9 1.6 broadcast_in_dim.50
  54.5 12.8 %while.31 = (s32[]{:T(128)}, f32[128,4,8,128]{3,0,2,1:T(8,128)}, f32[512,4,128]{2,0,1:T(8,128)}, f32[512,4,128]{2,0,1:T(8,128)}, s32[]{:T(128)}, /*index=5*/bf16...) while((s32[]{:T(128)}, f32[128,4,8,128]{3,0,2,1:T(8,128)}, ...), condition=%wide.region_6.7_spmd.clone, body=%wide.region_5.6_spmd.clone.sunk | while | flops 2704478464 | bytes 94034632 | solution.py:158
  54.5 0.6 iota_compare_fusion.6
  55.4 3.4 fusion.99
  58.8 1.3 fusion.102
  60.2 1.3 fusion.100
  61.8 1.5 fusion.101
  63.5 2.4 bitcast_add_fusion.2
  65.9 1.4 copy-done.2
  67.2 2.3 copy_bitcast_fusion.1
  69.6 25.8 %reduce-scatter.7.cloned.1.call-done = f32[128,512]{1,0:T(8,128)} async-done(((f32[512,512]{1,0:T(8,128)}), f32[128,512]{1,0:T(8,128)}) %reduce-scatter.7.cloned.1.call-update) | async-done | bytes 262160 | tf_op jit(solution)/shard_map/reduce_scatter | solution.py:173
  95.4 1.0 convert_element_type.49
  96.4 8.1 %convolution_bitcast_fusion.1 = f32[8192,512]{0,1:T(8,128)} fusion(bf16[128,512]{1,0:T(8,128)(2,1)S(1)} %convert_element_type.49, bf16[128,8192]{1,0:T(8,128)(2,1)S(1)} %copy-done), kind=kOutput, calls=%fused_computation.58 | convolution fusion | flops 1073741824 | bytes 19005440 | tf_op jit(solution)/shard_map/dot_general | solution.py:197
  104.6 1.1 copy-done.8
  105.8 1.3 copy.35
  107.4 122.3 %reduce-scatter.9.cloned.1.call-done = f32[2048,512]{0,1:T(8,128)} async-done(((f32[8192,512]{0,1:T(8,128)}), f32[2048,512]{0,1:T(8,128)}) %reduce-scatter.9.cloned.1.call-update) | async-done | bytes 4194320 | tf_op jit(solution)/shard_map/reduce_scatter | solution.py:196
  229.8 3.0 fusion.47
  232.8 2.7 subtract_convert_fusion
  235.5 0.6 pad_maximum_fusion.1
  236.1 1.4 copy.58
  237.5 19.5 %reduce-scatter.5.cloned.1.call-done = f32[128,512]{0,1:T(8,128)} async-done(((f32[512,512]{0,1:T(8,128)}), f32[128,512]{0,1:T(8,128)}) %reduce-scatter.5.cloned.1.call-update) | async-done | bytes 262160 | tf_op jit(solution)/shard_map/reduce_scatter | solution.py:167
  257.0 1.0 subtract_convert_fusion.2
  258.1 0.8 copy.45
  258.8 90.6 %reduce-scatter.11.cloned.1.call-done = f32[2048,64]{0,1:T(8,128)} async-done(((f32[2048,512]{0,1:T(8,128)}), f32[2048,64]{0,1:T(8,128)}) %reduce-scatter.11.cloned.1.call-update) | async-done | bytes 524304 | tf_op jit(solution)/shard_map/reduce_scatter | solution.py:204
  (70 shorter events, 2.8 us)
Async XLA Ops:
  7.2 89.2 %copy-start = (bf16[128,8192]{1,0:T(8,128)(2,1)S(1)}, bf16[128,8192]{1,0:T(8,128)(2,1)}, u32[]{:S(2)}) copy-start(bf16[128,8192]{1,0:T(8,128)(2,1)} %param.17) | copy-start | bytes 6291460
  7.2 88.3 %reduce-scatter.7.cloned.1.call-start = ((), (), s32[]{:S(2)}) async-start(), calls=%async_computation.5 | async-start | bytes 1310720 | tf_op jit(solution)/shard_map/reduce_scatter | solution.py:173
  17.9 2.3 copy-start.16
  18.0 22.9 %copy-start.13 = (f32[128,64]{1,0:T(8,128)}, f32[128,64]{1,0:T(8,128)S(1)}, u32[]{:S(2)}) copy-start(f32[128,64]{1,0:T(8,128)S(1)} %copy.20) | copy-start | bytes 98308
  46.5 1.8 copy-start.3
  46.5 1.8 copy-start.11
  55.4 3.4 copy-start.4
  55.4 3.4 copy-start.9
  58.8 1.3 copy-start.12
  60.2 1.3 copy-start.10
  60.2 1.6 copy-start.6
  61.8 1.6 copy-start.1
  61.8 1.7 copy-start.5
  63.5 2.4 copy-start.7
  65.9 1.4 copy-start.2
  69.6 160.1 %reduce-scatter.9.cloned.1.call-start = ((), (), s32[]{:S(2)}) async-start(), calls=%async_computation.6 | async-start | bytes 20971520 | tf_op jit(solution)/shard_map/reduce_scatter | solution.py:196
  96.4 8.1 %copy-start.15 = (bf16[128,512]{1,0:T(8,128)(2,1)}, bf16[128,512]{1,0:T(8,128)(2,1)S(1)}, u32[]{:S(2)}) copy-start(bf16[128,512]{1,0:T(8,128)(2,1)S(1)} %convert_element_type.49) | copy-start | bytes 393220
  104.5 1.2 copy-start.8
  104.6 125.1 %copy-start.18 = (f32[128,64]{0,1:T(8,128)S(1)}, f32[128,64]{0,1:T(8,128)}, u32[]{:S(2)}) copy-start(f32[128,64]{0,1:T(8,128)} %get-tuple-element.322) | copy-start | bytes 98308
  104.6 152.4 %reduce-scatter.5.cloned.1.call-start = ((), (), s32[]{:S(2)}) async-start(), calls=%async_computation.4 | async-start | bytes 1310720 | tf_op jit(solution)/shard_map/reduce_scatter | solution.py:167
  107.1 242.3 %reduce-scatter.11.cloned.1.call-start = ((), (), s32[]{:S(2)}) async-start(), calls=%async_computation.7 | async-start | bytes 4718592 | tf_op jit(solution)/shard_map/reduce_scatter | solution.py:204
  229.8 3.0 copy-start.14
  235.5 21.5 %copy-start.17 = (f32[128,64]{0,1:T(8,128)S(1)}, f32[128,64]{0,1:T(8,128)}, u32[]{:S(2)}) copy-start(f32[128,64]{0,1:T(8,128)} %copy-done.16) | copy-start | bytes 98308
Sparse Core Ops, SparseCore 0:
  69.7 25.6 reduce-scatter.6
  104.7 124.9 reduce-scatter.8
  232.2 24.7 reduce-scatter.4
  261.1 88.2 reduce-scatter.10
where the time goes:
time: 357 us; the launch traced here: 356 us
  waiting for transfers between devices  258 us (72%)
  local copies, waits for them, and re-layouts  26.1 us (7%)
  matrix products  22.7 us (6%)
  blocking collectives  20.3 us (6%)
  between operations  14.8 us (4%)
  other arithmetic  13.3 us (4%)
    reduce_scatter x1, waiting for transfers between devices, per_device(): lax.psum_scatter(lax.dot_general(inputs, value_grad, (((0,), (0,)), ((),...  122 us
    reduce_scatter x1, waiting for transfers between devices, per_device(): lax.psum_scatter(weight_part, 'dp', scatter_dimension=1, tiled=True)  90.6 us
    reduce_scatter x1, waiting for transfers between devices, per_device(): lax.psum_scatter(value_accumulator.reshape(retained_slots, KEY_HEADS * HE...  25.8 us
    reduce_scatter x1, waiting for transfers between devices, per_device(): lax.psum_scatter(key_accumulator.reshape(retained_slots, KEY_HEADS * HEAD...  19.5 us
    unnamed x26, local copies, waits for them, and re-layouts  10.9 us
    dot_general x1, matrix products, per_device(): lax.dot_general(inputs, value_grad, (((0,), (0,)), ((), ())), preferred_e...  8.12 us
    all_gather x1, blocking collectives, per_device(): lax.all_gather(value_head_inputs, 'ctx', axis=0, tiled=True)  7.29 us
  transfers between devices with their start and end apart: 4, of which 4 were waited for; matrix products, arithmetic and copies ran while one was open for 3% of the time, Pallas kernels for 0%

commit v1 on v0

--- a/solution.py
+++ b/solution.py
@@ -48,6 +48,7 @@
     my_index = lax.axis_index("ctx")
     score_scale = 1.0 / math.sqrt(HEAD_DIM)
     cosine_table, sine_lookup = rope_tables(positions, HEAD_DIM)
+    column_inputs = lax.all_to_all(inputs, "ctx", 1, 0, tiled=True)
     query_rotated = apply_rotation(
         queries.reshape(row_number_total, QUERY_HEADS, HEAD_DIM).astype(jnp.float32),
         cosine_table,
@@ -193,16 +194,12 @@
         .reshape(row_number_total, KEY_HEADS * HEAD_DIM)
     )
     value_grad = value_part.astype(jnp.bfloat16)
-    weight_part = lax.psum_scatter(
-        lax.dot_general(
-            inputs, value_grad, (((0,), (0,)), ((), ())), preferred_element_type=jnp.float32
-        ),
-        "ctx",
-        scatter_dimension=0,
-        tiled=True,
-    )
-    shares = lax.psum_scatter(weight_part, "dp", scatter_dimension=1, tiled=True)
-    return (query_grad, key_grad, value_grad, shares.T)
+    sequence_grad = lax.all_gather(value_grad, "ctx", axis=0, tiled=True)
+    weight_part = lax.dot_general(
+        sequence_grad, column_inputs, (((0,), (0,)), ((), ())), preferred_element_type=jnp.float32
+    )
+    shares = lax.psum_scatter(weight_part, "dp", scatter_dimension=0, tiled=True)
+    return (query_grad, key_grad, value_grad, shares)
 
 
 def solution(mesh):

time: 357 us -> 226 us (0.63)
  waiting for transfers between devices: 258 us -> 117 us
  blocking collectives: 20.3 us -> 26.6 us
  starting transfers between devices: 0.38 us -> 4.58 us
    reduce_scatter x2 -> x1, waiting for transfers between devices: 213 us -> 87.3 us  [per_device(): lax.psum_scatter(weight_part, 'dp', scatter_dimension=0, tiled=True)]
    all_to_all x0 -> x1, waiting for transfers between devices: none -> 29.9 us  [per_device(): column_inputs = lax.all_to_all(inputs, 'ctx', 1, 0, tiled=True)]
    reduce_scatter x1, waiting for transfers between devices: 25.8 us -> 0.01 us  [per_device(): lax.psum_scatter(value_accumulator.reshape(retained_slots, KEY_HEADS * HE...]
    reduce_scatter x1, waiting for transfers between devices: 19.5 us -> 0.01 us  [per_device(): lax.psum_scatter(key_accumulator.reshape(retained_slots, KEY_HEADS * HEAD...]
    all_gather x0 -> x1, blocking collectives: none -> 6.72 us  [per_device(): sequence_grad = lax.all_gather(value_grad, 'ctx', axis=0, tiled=True)]
    all_to_all x0 -> x1, starting transfers between devices: none -> 4.46 us  [per_device(): column_inputs = lax.all_to_all(inputs, 'ctx', 1, 0, tiled=True)]
    all_to_all x0 -> x1, local copies, waits for them, and re-layouts: none -> 4.02 us  [per_device(): column_inputs = lax.all_to_all(inputs, 'ctx', 1, 0, tiled=True)]
    unnamed x26 -> x39, local copies, waits for them, and re-layouts: 10.9 us -> 10.7 us
  transfers between devices with their start and end apart: 4 -> 4, of which waited for: 4 -> 2; matrix products, arithmetic and copies ran while one was open for 3% -> 10% of each run, Pallas kernels for 0% -> 0%
where the time goes in v1:
time: 226 us; the launch traced here: 225 us
  waiting for transfers between devices  117 us (52%)
  blocking collectives  26.6 us (12%)
  local copies, waits for them, and re-layouts  26.4 us (12%)
  matrix products  20.6 us (9%)
  other arithmetic  14.8 us (7%)
  between operations  14.8 us (7%)
  starting transfers between devices  4.58 us (2%)
    reduce_scatter x1, waiting for transfers between devices, per_device(): lax.psum_scatter(weight_part, 'dp', scatter_dimension=0, tiled=True)  87.3 us
    all_to_all x1, waiting for transfers between devices, per_device(): column_inputs = lax.all_to_all(inputs, 'ctx', 1, 0, tiled=True)  29.9 us
    unnamed x39, local copies, waits for them, and re-layouts  10.7 us
    all_gather x1, blocking collectives, per_device(): lax.all_gather(key_rotated, 'ctx', axis=0, tiled=True)  8.65 us
    all_gather x1, blocking collectives, per_device(): sequence_grad = lax.all_gather(value_grad, 'ctx', axis=0, tiled=True)  6.72 us
    all_gather x1, blocking collectives, per_device(): lax.all_gather(value_head_inputs, 'ctx', axis=0, tiled=True)  6.62 us
    dot_general x1, matrix products, per_device(): lax.dot_general(sequence_grad, column_inputs, (((0,), (0,)), ((), ())), p...  4.9 us
    dot_general x2, matrix products, scores_for(): jnp.einsum('qhgd,khd->hgqk', query_grouped, k_blk, preferred_element_type...  4.61 us
  transfers between devices with their start and end apart: 4, of which 2 were waited for; matrix products, arithmetic and copies ran while one was open for 10% of the time, Pallas kernels for 0%

profile of v1, /device:TPU:0, one launch (start us, length us, event | category | flops | bytes accessed | tf_op | source)
XLA Modules:
  0.0 225.2 jit_solution(14194657916298984292)
XLA Ops:
  7.2 0.7 convert_element_type.43
  7.9 0.8 broadcast_multiply_fusion
  8.9 1.4 convert_bitcast_fusion
  10.3 0.4 copy.73
  10.7 0.8 subtract_convert_fusion.1
  11.6 1.4 copy.43
  13.0 1.4 copy.44
  14.6 8.6 %all_gather.13 = bf16[512,512]{0,1:T(8,128)(2,1)S(1)} all-gather(bf16[128,512]{0,1:T(8,128)(2,1)S(1)} %bitcast.177), channel_id=1, replica_groups=mesh['dp'=8,'ctx'=4] {'ctx'}, dimensions={0}, use_global_device_ids=true | all-gather | bytes 655360 | tf_op jit(solution)/shard_map/all_gather | solution.py:66
  23.9 0.6 dynamic-slice
  24.5 0.7 dynamic-update-slice
  25.2 0.3 copy.50
  25.5 4.6 %all-reduce = s32[4]{0:T(128)S(1)} all-reduce(s32[4]{0:T(128)S(1)} %dynamic-update-slice), channel_id=1, replica_groups=mesh['dp'=8,'ctx'=4] {'ctx'}, use_global_device_ids=true, to_apply=%add | all-reduce | flops 4 | bytes 32
  30.1 0.7 copy.46
  30.8 0.7 copy.49
  31.6 6.6 %all_gather.14 = bf16[512,512]{0,1:T(8,128)(2,1)S(1)} all-gather(bf16[128,512]{0,1:T(8,128)(2,1)S(1)} %copy.45), channel_id=1, replica_groups=mesh['dp'=8,'ctx'=4] {'ctx'}, dimensions={0}, use_global_device_ids=true | all-gather | bytes 655360 | tf_op jit(solution)/shard_map/all_gather | solution.py:67
  38.5 2.1 pad_maximum_fusion
  40.6 6.5 %while.30 = (s32[]{:T(128)}, f32[4,8,128]{2,1,0:T(8,128)S(1)}, f32[4,8,128]{2,1,0:T(8,128)S(1)}, f32[4,8,128]{2,1,0:T(8,128)S(1)}, s32[]{:T(128)}, /*index=5*/bf...) while((s32[]{:T(128)}, f32[4,8,128]{2,1,0:T(8,128)S(1)}, ...), condition=%wide.region_4.5_spmd.clone, body=%wide.region_0.4_spmd.clone.sunk | while | flops 1099120896 | bytes 28875180 | solution.py:121
  40.7 0.6 iota_compare_fusion.5
  41.6 1.3 fusion.86
  42.9 2.4 %fusion.87 = f32[4,8,128]{2,1,0:T(8,128)S(1)} fusion(f32[4,512,128,8]{2,1,3,0:T(8,128)S(1)} %get-tuple-element.508, f32[4,8,128]{2,1,0:T(8,128)S(1)} %max.5, pred[128,512]{0,1:T(8,128)(4,1)S(1)} %compare_and_fusion.4, bf16[128,4,8,128]{3,0,2,1:T(8,128)(2,1)S(1)} %get-tuple-element.562, bf16[512,4,128]{2,0,1:T(8,128)(2,1)S(1)} %get-tuple-element.561), kind=kOutput, calls=%fused_computation.7.clone.1 | convolution fusion | flops 547352576 | bytes 10059776 | tf_op jit(solution)/shard_map/while/body/qhgd,khd->hgqk/dot_general | solution.py:98
  45.4 1.8 fusion.88
  47.2 0.9 copy-done
  48.7 1.0 broadcast_in_dim.66
  49.8 1.1 broadcast_in_dim.66.clone
  50.9 14.0 %while.31 = (s32[]{:T(128)}, f32[128,4,8,128]{3,0,2,1:T(8,128)S(1)}, f32[512,4,128]{2,0,1:T(8,128)}, f32[512,4,128]{2,0,1:T(8,128)}, s32[]{:T(128)}, /*index=5*/...) while((s32[]{:T(128)}, ...), condition=%wide.region_6.7_spmd.clone, body=%wide.region_5.6_spmd.clone.sunk | while | flops 2704478464 | bytes 68868688 | solution.py:159
  50.9 0.6 iota_compare_fusion.6
  51.8 3.3 %fusion.100 = f32[4,8,128,512]{2,3,1,0:T(8,128)S(1)} fusion(f32[4,8,128]{2,1,0:T(8,128)S(1)} %get-tuple-element.610, f32[4,8,128]{2,1,0:T(8,128)S(1)} %get-tuple-element.609, pred[128,512]{0,1:T(8,128)(4,1)S(1)} %compare_and_fusion.5, bf16[128,4,8,128]{3,0,2,1:T(8,128)(2,1)S(1)} %get-tuple-element.608, bf16[512,4,128]{2,0,1:T(8,128)(2,1)} %get-tuple-element.607), kind=kOutput, calls=%fused_computation.37.clone.1 | convolution fusion | flops 545259520 | bytes 10059776 | tf_op jit(solution)/shard_map/while/body/qhgd,khd->hgqk/dot_general | solution.py:95
  55.2 1.3 fusion.101
  56.5 2.4 %bitcast_add_fusion.2 = f32[128,4,8,128]{3,0,2,1:T(8,128)S(1)} fusion(f32[128,4,8,128]{3,0,2,1:T(8,128)S(1)} %get-tuple-element.586, bf16[4,8,128,512]{2,3,1,0:T(8,128)(2,1)S(1)} %fusion.101, bf16[512,4,128]{2,0,1:T(8,128)(2,1)S(1)} %copy-done.3), kind=kOutput, calls=%fused_computation.40.clone.1 | convolution fusion | flops 537395200 | bytes 8912896 | tf_op jit(solution)/shard_map/while/body/hgqk,khd->qhgd/dot_general | solution.py:135
  58.9 1.5 fusion.102
  60.4 1.0 copy-done.5
  61.3 3.5 %fusion.103 = f32[512,4,128]{2,0,1:T(8,128)} fusion(f32[512,4,128]{2,0,1:T(8,128)} %get-tuple-element.588, bf16[128,4,8,128]{3,0,2,1:T(8,128)(2,1)S(1)} %copy-done.1, f32[4,8,128,512]{2,3,1,0:T(8,128)S(1)} %fusion.100), kind=kOutput, calls=%fused_computation.43.clone.1 | convolution fusion | flops 539230208 | bytes 11534336 | tf_op jit(solution)/shard_map/while/body/hgqk,qhgd->khd/dot_general | solution.py:141
  64.9 2.3 %copy_bitcast_fusion.1 = f32[512,512]{1,0:T(8,128)} fusion(f32[512,4,128]{2,0,1:T(8,128)} %get-tuple-element.154), kind=kLoop, calls=%fused_computation.64 | loop fusion | bytes 2097152 | tf_op jit(solution)/shard_map/reshape | solution.py:175
  67.2 4.2 %copy.59 = bf16[128,8192]{0,1:T(8,128)(2,1)} copy(bf16[128,8192]{1,0:T(8,128)(2,1)} %param.17) | data formatting | bytes 4194304 | tf_op args[6]
  71.4 4.5 %all-to-all-start = ((bf16[128,4,2048]{0,2,1:T(8,128)(2,1)}), bf16[128,4,2048]{0,2,1:T(8,128)(2,1)}, u32[]{:S(2)}, u32[]{:S(2)}) async-start(bf16[128,4,2048]{0,2,1:T(8,128)(2,1)} %bitcast.166), calls=%async_computation.2 | async-start | bytes 4194304 | tf_op jit(solution)/shard_map/all_to_all | solution.py:51
  76.0 1.3 copy.56
  77.3 29.9 %all-to-all-done = bf16[128,4,2048]{0,2,1:T(8,128)(2,1)} async-done(((bf16[128,4,2048]{0,2,1:T(8,128)(2,1)}), bf16[128,4,2048]{0,2,1:T(8,128)(2,1)}, u32[]{:S(2)}, u32[]{:S(2)}) %all-to-all-start) | async-done | bytes 2097184 | tf_op jit(solution)/shard_map/all_to_all | solution.py:51
  107.2 4.0 %copy.60 = bf16[4,128,2048]{2,1,0:T(8,128)(2,1)} copy(bf16[4,128,2048]{1,2,0:T(8,128)(2,1)} %bitcast.13) | data formatting | bytes 4194304 | tf_op jit(solution)/shard_map/all_to_all | solution.py:51
  111.3 1.0 convert_element_type.49
  112.2 6.7 %all_gather.15 = bf16[512,512]{1,0:T(8,128)(2,1)S(1)} all-gather(bf16[128,512]{1,0:T(8,128)(2,1)S(1)} %convert_element_type.49), channel_id=1, replica_groups=mesh['dp'=8,'ctx'=4] {'ctx'}, dimensions={0}, use_global_device_ids=true | all-gather | bytes 655360 | tf_op jit(solution)/shard_map/all_gather | solution.py:197
  119.0 4.9 %fusion.48 = f32[512,2048]{1,0:T(8,128)} fusion(bf16[512,512]{1,0:T(8,128)(2,1)S(1)} %all_gather.15, bf16[512,2048]{1,0:T(8,128)(2,1)} %bitcast.167), kind=kOutput, calls=%fused_computation.81 | convolution fusion | flops 1073741824 | bytes 6815744 | tf_op jit(solution)/shard_map/dot_general | solution.py:198
  124.0 0.7 fusion.47
  124.8 2.7 %subtract_convert_fusion = (bf16[128,32,64]{2,1,0:T(8,128)(2,1)S(1)}, bf16[128,32,64]{2,1,0:T(8,128)(2,1)S(1)}) fusion(f32[128,32,64]{2,0,1:T(8,128)S(1)} %get-tuple-element.344, f32[128,32,64]{2,0,1:T(8,128)S(1)} %get-tuple-element.343, f32[128,64]{1,0:T(8,128)S(1)} %copy.55, f32[128,64]{1,0:T(8,128)S(1)} %copy-done.11), kind=kLoop, calls=%fused_computation.60 | loop fusion | flops 2097152 | bytes 3211264 | tf_op jit(solution)/shard_map/convert.4
  127.6 0.6 pad_maximum_fusion.1
  128.1 1.4 copy.81
  129.6 1.0 subtract_convert_fusion.2
  130.6 0.8 copy.68
  131.4 87.3 %reduce-scatter.8.cloned.1.call-done = f32[64,2048]{1,0:T(8,128)} async-done(((f32[512,2048]{1,0:T(8,128)}), f32[64,2048]{1,0:T(8,128)}) %reduce-scatter.8.cloned.1.call-update) | async-done | bytes 524304 | tf_op jit(solution)/shard_map/reduce_scatter | solution.py:201
  (72 shorter events, 2.4 us)
Async XLA Ops:
  7.2 104.1 %reduce-scatter.6.cloned.1.call-start = ((), (), s32[]{:S(2)}) async-start(), calls=%async_computation.5 | async-start | bytes 1310720 | tf_op jit(solution)/shard_map/reduce_scatter | solution.py:174
  8.7 5.8 %copy-start.12 = (f32[128,64]{0,1:T(8,128)}, f32[128,64]{0,1:T(8,128)S(1)}, u32[]{:S(2)}) copy-start(f32[128,64]{0,1:T(8,128)S(1)} %get-tuple-element.351) | copy-start | bytes 98308
  8.8 2.7 %copy-start.10 = (f32[128,64]{1,0:T(8,128)}, f32[128,64]{1,0:T(8,128)S(1)}, u32[]{:S(2)}) copy-start(f32[128,64]{1,0:T(8,128)S(1)} %copy.41) | copy-start | bytes 98308
  10.7 3.6 %copy-start.16 = (bf16[128,512]{1,0:T(8,128)(2,1)S(1)}, bf16[128,512]{1,0:T(8,128)(2,1)}, u32[]{:S(2)}) copy-start(bf16[128,512]{1,0:T(8,128)(2,1)} %param.12) | copy-start | bytes 393220
  11.5 12.3 %copy-start.18 = (u32[32]{0:T(128)S(1)}, u32[32]{0:T(128)}, u32[]{:S(2)}) copy-start(u32[32]{0:T(128)} %constant.76) | copy-start | bytes 388
  11.6 18.6 %copy-start.9 = (bf16[128,4096]{1,0:T(8,128)(2,1)S(1)}, bf16[128,4096]{1,0:T(8,128)(2,1)}, u32[]{:S(2)}) copy-start(bf16[128,4096]{1,0:T(8,128)(2,1)} %param.14) | copy-start | bytes 3145732
  13.0 18.5 %copy-start.17 = (bf16[128,512]{1,0:T(8,128)(2,1)S(1)}, bf16[128,512]{1,0:T(8,128)(2,1)}, u32[]{:S(2)}) copy-start(bf16[128,512]{1,0:T(8,128)(2,1)} %param.13) | copy-start | bytes 393220
  47.2 1.0 copy-start
  47.2 1.1 copy-start.2
  47.2 1.3 copy-start.7
  51.8 3.4 %copy-start.1 = (bf16[128,4,8,128]{3,0,2,1:T(8,128)(2,1)S(1)}, bf16[128,4,8,128]{3,0,2,1:T(8,128)(2,1)}, u32[]{:S(2)}) copy-start(bf16[128,4,8,128]{3,0,2,1:T(8,128)(2,1)} %get-tuple-element.612) | copy-start | bytes 3145732 | tf_op jit(solution)/shard_map/while
  51.8 3.4 %copy-start.8 = (bf16[512,4,128]{2,0,1:T(8,128)(2,1)S(1)}, bf16[512,4,128]{2,0,1:T(8,128)(2,1)}, u32[]{:S(2)}) copy-start(bf16[512,4,128]{2,0,1:T(8,128)(2,1)} %get-tuple-element.611) | copy-start | bytes 1572868 | tf_op jit(solution)/shard_map/while
  55.2 1.3 copy-start.3
  56.5 2.4 %copy-start.4 = (f32[512,4,128]{2,0,1:T(8,128)S(1)}, f32[512,4,128]{2,0,1:T(8,128)}, u32[]{:S(2)}) copy-start(f32[512,4,128]{2,0,1:T(8,128)} %get-tuple-element.587) | copy-start | bytes 3145732 | tf_op jit(solution)/shard_map/while
  60.4 1.0 copy-start.5
  67.2 8.7 %copy-start.6 = (f32[512,4,128]{2,0,1:T(8,128)S(1)}, f32[512,4,128]{2,0,1:T(8,128)}, u32[]{:S(2)}) copy-start(f32[512,4,128]{2,0,1:T(8,128)} %get-tuple-element.153) | copy-start | bytes 3145732
  71.4 35.8 %all-to-all-start = ((bf16[128,4,2048]{0,2,1:T(8,128)(2,1)}), bf16[128,4,2048]{0,2,1:T(8,128)(2,1)}, u32[]{:S(2)}, u32[]{:S(2)}) async-start(bf16[128,4,2048]{0,2,1:T(8,128)(2,1)} %bitcast.166), calls=%async_computation.2 | async-start | bytes 4194304 | tf_op jit(solution)/shard_map/all_to_all | solution.py:51
  75.9 53.7 %reduce-scatter.4.cloned.1.call-start = ((), (), s32[]{:S(2)}) async-start(), calls=%async_computation.4 | async-start | bytes 1310720 | tf_op jit(solution)/shard_map/reduce_scatter | solution.py:168
  77.3 141.4 %reduce-scatter.8.cloned.1.call-start = ((), (), s32[]{:S(2)}) async-start(), calls=%async_computation.6 | async-start | bytes 4718592 | tf_op jit(solution)/shard_map/reduce_scatter | solution.py:201
  112.2 11.7 %copy-start.14 = (bf16[128,512]{1,0:T(8,128)(2,1)}, bf16[128,512]{1,0:T(8,128)(2,1)S(1)}, u32[]{:S(2)}) copy-start(bf16[128,512]{1,0:T(8,128)(2,1)S(1)} %convert_element_type.49) | copy-start | bytes 393220
  119.0 4.9 %copy-start.15 = (f32[128,64]{0,1:T(8,128)S(1)}, f32[128,64]{0,1:T(8,128)}, u32[]{:S(2)}) copy-start(f32[128,64]{0,1:T(8,128)} %get-tuple-element.349) | copy-start | bytes 98308
  124.0 0.8 copy-start.11
  127.6 2.0 copy-start.13
Sparse Core Ops, SparseCore 0:
  67.4 31.4 reduce-scatter.5
  101.4 24.7 reduce-scatter.3
  130.4 88.2 reduce-scatter.7

commit v2 on v1

--- a/solution.py
+++ b/solution.py
@@ -198,7 +198,15 @@
     weight_part = lax.dot_general(
         sequence_grad, column_inputs, (((0,), (0,)), ((), ())), preferred_element_type=jnp.float32
     )
-    shares = lax.psum_scatter(weight_part, "dp", scatter_dimension=0, tiled=True)
+    dp_span = lax.axis_size("dp")
+    pieces = lax.all_to_all(
+        weight_part.reshape(dp_span, weight_part.shape[0] // dp_span, weight_part.shape[1]),
+        "dp",
+        0,
+        0,
+        tiled=True,
+    )
+    shares = jnp.sum(pieces, axis=0)
     return (query_grad, key_grad, value_grad, shares)
 
 

time: 226 us -> 225 us (level)
  waiting for transfers between devices: 117 us -> 109 us
  starting transfers between devices: 4.58 us -> 10.7 us
  local copies, waits for them, and re-layouts: 26.4 us -> 21.6 us
  other arithmetic: 14.8 us -> 18.1 us
  blocking collectives: 26.6 us -> 29.8 us
    reduce_scatter x1 -> x0, waiting for transfers between devices: 87.3 us -> none  [per_device(): lax.psum_scatter(weight_part, 'dp', scatter_dimension=0, tiled=True)]
    all_to_all x0 -> x1, waiting for transfers between devices: none -> 63.4 us  [per_device(): lax.all_to_all(weight_part.reshape(dp_span, weight_part.shape[0] // dp_sp...]
    all_to_all x1, waiting for transfers between devices: 29.9 us -> 0.01 us  [per_device(): column_inputs = lax.all_to_all(inputs, 'ctx', 1, 0, tiled=True)]
    reduce_scatter x1, waiting for transfers between devices: 0.01 us -> 23.9 us  [per_device(): lax.psum_scatter(value_accumulator.reshape(retained_slots, KEY_HEADS * HE...]
    reduce_scatter x1, waiting for transfers between devices: 0.01 us -> 21.2 us  [per_device(): lax.psum_scatter(key_accumulator.reshape(retained_slots, KEY_HEADS * HEAD...]
    all_to_all x0 -> x1, starting transfers between devices: none -> 5.98 us  [per_device(): lax.all_to_all(weight_part.reshape(dp_span, weight_part.shape[0] // dp_sp...]
    unnamed x39 -> x38, local copies, waits for them, and re-layouts: 10.7 us -> 6.54 us
    reduce_sum x0 -> x1, other arithmetic: none -> 3.27 us  [per_device(): shares = jnp.sum(pieces, axis=0)]
  transfers between devices with their start and end apart: 4 -> 4, of which waited for: 2 -> 3; matrix products, arithmetic and copies ran while one was open for 10% -> 6% of each run, Pallas kernels for 0% -> 0%
where the time goes in v2:
time: 225 us
  waiting for transfers between devices  109 us (48%)
  blocking collectives  29.8 us (13%)
  local copies, waits for them, and re-layouts  21.6 us (10%)
  matrix products  20.5 us (9%)
  other arithmetic  18.1 us (8%)
  between operations  15.1 us (7%)
  starting transfers between devices  10.7 us (5%)
    all_to_all x1, waiting for transfers between devices, per_device(): lax.all_to_all(weight_part.reshape(dp_span, weight_part.shape[0] // dp_sp...  63.4 us
    reduce_scatter x1, waiting for transfers between devices, per_device(): lax.psum_scatter(value_accumulator.reshape(retained_slots, KEY_HEADS * HE...  23.9 us
    reduce_scatter x1, waiting for transfers between devices, per_device(): lax.psum_scatter(key_accumulator.reshape(retained_slots, KEY_HEADS * HEAD...  21.2 us
    all_gather x1, blocking collectives, per_device(): sequence_grad = lax.all_gather(value_grad, 'ctx', axis=0, tiled=True)  9.98 us
    all_gather x1, blocking collectives, per_device(): lax.all_gather(key_rotated, 'ctx', axis=0, tiled=True)  8.65 us
    all_gather x1, blocking collectives, per_device(): lax.all_gather(value_head_inputs, 'ctx', axis=0, tiled=True)  6.62 us
    unnamed x38, local copies, waits for them, and re-layouts  6.54 us
    all_to_all x1, starting transfers between devices, per_device(): lax.all_to_all(weight_part.reshape(dp_span, weight_part.shape[0] // dp_sp...  5.98 us
  transfers between devices with their start and end apart: 4, of which 3 were waited for; matrix products, arithmetic and copies ran while one was open for 6% of the time, Pallas kernels for 0%

profile of v2, /device:TPU:0, one launch (start us, length us, event | category | flops | bytes accessed | tf_op | source)
XLA Modules:
  0.0 224.6 jit_solution(6058666184541787229)
XLA Ops:
  7.2 0.7 convert_element_type.43
  7.9 0.8 broadcast_multiply_fusion
  8.9 1.4 convert_bitcast_fusion
  10.7 0.8 subtract_convert_fusion.1
  11.6 1.4 copy.24
  13.0 1.4 copy.25
  14.5 8.6 %all_gather.13 = bf16[512,512]{0,1:T(8,128)(2,1)S(1)} all-gather(bf16[128,512]{0,1:T(8,128)(2,1)S(1)} %bitcast.187), channel_id=1, replica_groups=mesh['dp'=8,'ctx'=4] {'ctx'}, dimensions={0}, use_global_device_ids=true | all-gather | bytes 655360 | tf_op jit(solution)/shard_map/all_gather | solution.py:66
  23.8 0.7 dynamic-slice
  24.5 0.7 dynamic-update-slice
  25.5 4.6 %all-reduce = s32[4]{0:T(128)S(1)} all-reduce(s32[4]{0:T(128)S(1)} %dynamic-update-slice), channel_id=1, replica_groups=mesh['dp'=8,'ctx'=4] {'ctx'}, use_global_device_ids=true, to_apply=%add | all-reduce | flops 4 | bytes 32
  30.1 0.7 copy.27
  30.8 0.7 copy.30
  31.6 6.6 %all_gather.14 = bf16[512,512]{0,1:T(8,128)(2,1)S(1)} all-gather(bf16[128,512]{0,1:T(8,128)(2,1)S(1)} %copy.26), channel_id=1, replica_groups=mesh['dp'=8,'ctx'=4] {'ctx'}, dimensions={0}, use_global_device_ids=true | all-gather | bytes 655360 | tf_op jit(solution)/shard_map/all_gather | solution.py:67
  38.5 2.1 pad_maximum_fusion
  40.6 6.6 %while.30 = (s32[]{:T(128)}, f32[4,8,128]{2,1,0:T(8,128)S(1)}, f32[4,8,128]{2,1,0:T(8,128)S(1)}, f32[4,8,128]{2,1,0:T(8,128)S(1)}, s32[]{:T(128)}, /*index=5*/bf...) while((s32[]{:T(128)}, f32[4,8,128]{2,1,0:T(8,128)S(1)}, ...), condition=%wide.region_4.5_spmd.clone, body=%wide.region_0.4_spmd.clone.sunk | while | flops 1099120896 | bytes 28875180 | solution.py:121
  40.7 0.6 iota_compare_fusion.5
  41.6 1.3 fusion.86
  42.9 2.5 %fusion.87 = f32[4,8,128]{2,1,0:T(8,128)S(1)} fusion(f32[4,512,128,8]{2,1,3,0:T(8,128)S(1)} %get-tuple-element.481, f32[4,8,128]{2,1,0:T(8,128)S(1)} %max.5, pred[128,512]{0,1:T(8,128)(4,1)S(1)} %compare_and_fusion.4, bf16[128,4,8,128]{3,0,2,1:T(8,128)(2,1)S(1)} %get-tuple-element.535, bf16[512,4,128]{2,0,1:T(8,128)(2,1)S(1)} %get-tuple-element.534), kind=kOutput, calls=%fused_computation.7.clone.1 | convolution fusion | flops 547352576 | bytes 10059776 | tf_op jit(solution)/shard_map/while/body/qhgd,khd->hgqk/dot_general | solution.py:98
  45.4 1.8 fusion.88
  47.2 0.9 copy-done
  48.7 1.0 broadcast_in_dim.66
  49.8 1.1 broadcast_in_dim.66.clone
  50.8 14.0 %while.31 = (s32[]{:T(128)}, f32[128,4,8,128]{3,0,2,1:T(8,128)S(1)}, f32[512,4,128]{2,0,1:T(8,128)}, f32[512,4,128]{2,0,1:T(8,128)}, s32[]{:T(128)}, /*index=5*/...) while((s32[]{:T(128)}, ...), condition=%wide.region_6.7_spmd.clone, body=%wide.region_5.6_spmd.clone.sunk | while | flops 2704478464 | bytes 68868688 | solution.py:159
  50.9 0.6 iota_compare_fusion.6
  51.8 3.3 %fusion.100 = f32[4,8,128,512]{2,3,1,0:T(8,128)S(1)} fusion(f32[4,8,128]{2,1,0:T(8,128)S(1)} %get-tuple-element.583, f32[4,8,128]{2,1,0:T(8,128)S(1)} %get-tuple-element.582, pred[128,512]{0,1:T(8,128)(4,1)S(1)} %compare_and_fusion.5, bf16[128,4,8,128]{3,0,2,1:T(8,128)(2,1)S(1)} %get-tuple-element.581, bf16[512,4,128]{2,0,1:T(8,128)(2,1)} %get-tuple-element.580), kind=kOutput, calls=%fused_computation.37.clone.1 | convolution fusion | flops 545259520 | bytes 10059776 | tf_op jit(solution)/shard_map/while/body/qhgd,khd->hgqk/dot_general | solution.py:95
  55.2 1.3 fusion.101
  56.5 2.4 %bitcast_add_fusion.2 = f32[128,4,8,128]{3,0,2,1:T(8,128)S(1)} fusion(f32[128,4,8,128]{3,0,2,1:T(8,128)S(1)} %get-tuple-element.559, bf16[4,8,128,512]{2,3,1,0:T(8,128)(2,1)S(1)} %fusion.101, bf16[512,4,128]{2,0,1:T(8,128)(2,1)S(1)} %copy-done.3), kind=kOutput, calls=%fused_computation.40.clone.1 | convolution fusion | flops 537395200 | bytes 8912896 | tf_op jit(solution)/shard_map/while/body/hgqk,khd->qhgd/dot_general | solution.py:135
  58.9 1.5 fusion.102
  60.3 1.0 copy-done.5
  61.3 3.5 %fusion.103 = f32[512,4,128]{2,0,1:T(8,128)} fusion(f32[512,4,128]{2,0,1:T(8,128)} %get-tuple-element.561, bf16[128,4,8,128]{3,0,2,1:T(8,128)(2,1)S(1)} %copy-done.1, f32[4,8,128,512]{2,3,1,0:T(8,128)S(1)} %fusion.100), kind=kOutput, calls=%fused_computation.43.clone.1 | convolution fusion | flops 539230208 | bytes 11534336 | tf_op jit(solution)/shard_map/while/body/hgqk,qhgd->khd/dot_general | solution.py:141
  64.8 2.3 %copy_bitcast_fusion.2 = f32[512,512]{1,0:T(8,128)} fusion(f32[512,4,128]{2,0,1:T(8,128)} %get-tuple-element.154), kind=kLoop, calls=%fused_computation.65 | loop fusion | bytes 2097152 | tf_op jit(solution)/shard_map/reshape | solution.py:175
  67.2 3.2 %copy.64 = bf16[16,4,8,2048]{3,2,0,1:T(8,128)(2,1)} copy(bf16[16,4,8,2048]{3,2,1,0:T(8,128)(2,1)} %bitcast.184) | data formatting | bytes 4194304 | tf_op jit(solution)/shard_map/all_to_all | solution.py:51
  70.3 4.4 %all-to-all-start = ((bf16[128,4,2048]{2,0,1:T(8,128)(2,1)}), bf16[128,4,2048]{2,0,1:T(8,128)(2,1)}, u32[]{:S(2)}, u32[]{:S(2)}) async-start(bf16[128,4,2048]{2,0,1:T(8,128)(2,1)} %bitcast.174), calls=%async_computation.2 | async-start | bytes 4194304 | tf_op jit(solution)/shard_map/all_to_all | solution.py:51
  74.8 23.9 %reduce-scatter.5.cloned.1.call-done = f32[128,512]{1,0:T(8,128)} async-done(((f32[512,512]{1,0:T(8,128)}), f32[128,512]{1,0:T(8,128)}) %reduce-scatter.5.cloned.1.call-update) | async-done | bytes 262160 | tf_op jit(solution)/shard_map/reduce_scatter | solution.py:174
  98.7 1.0 convert_element_type.49
  99.7 10.0 %all_gather.15 = bf16[512,512]{1,0:T(8,128)(2,1)S(1)} all-gather(bf16[128,512]{1,0:T(8,128)(2,1)S(1)} %convert_element_type.49), channel_id=1, replica_groups=mesh['dp'=8,'ctx'=4] {'ctx'}, dimensions={0}, use_global_device_ids=true | all-gather | bytes 655360 | tf_op jit(solution)/shard_map/all_gather | solution.py:197
  109.9 4.8 %fusion.48 = f32[8,64,2048]{2,1,0:T(8,128)} fusion(bf16[8,64,512]{2,1,0:T(8,128)(2,1)S(1)} %bitcast.180, bf16[512,2048,1]{1,0,2:T(8,128)(2,1)} %bitcast.16), kind=kOutput, calls=%fused_computation.82 | convolution fusion | flops 1073741824 | bytes 6815744 | tf_op jit(solution)/shard_map/dot_general | solution.py:198
  114.7 6.0 %all-to-all-start.1 = ((f32[8,64,2048]{2,1,0:T(8,128)}), f32[8,64,2048]{2,1,0:T(8,128)}, u32[]{:S(2)}, u32[]{:S(2)}) async-start(f32[8,64,2048]{2,1,0:T(8,128)} %fusion.48), calls=%async_computation.3 | async-start | bytes 8388608 | tf_op jit(solution)/shard_map/all_to_all | solution.py:202
  121.0 1.4 copy.37
  122.5 0.7 fusion.47
  123.4 2.7 %subtract_convert_fusion = (bf16[128,32,64]{2,1,0:T(8,128)(2,1)S(1)}, bf16[128,32,64]{2,1,0:T(8,128)(2,1)S(1)}) fusion(f32[128,32,64]{2,0,1:T(8,128)S(1)} %get-tuple-element.317, f32[128,32,64]{2,0,1:T(8,128)S(1)} %get-tuple-element.316, f32[128,64]{1,0:T(8,128)S(1)} %copy.36, f32[128,64]{1,0:T(8,128)S(1)} %copy-done.11), kind=kLoop, calls=%fused_computation.61 | loop fusion | flops 2097152 | bytes 3211264 | tf_op jit(solution)/shard_map/convert.4
  126.1 0.6 pad_maximum_fusion.1
  126.7 1.4 copy.65
  128.1 21.2 %reduce-scatter.3.cloned.1.call-done = f32[128,512]{0,1:T(8,128)} async-done(((f32[512,512]{0,1:T(8,128)}), f32[128,512]{0,1:T(8,128)}) %reduce-scatter.3.cloned.1.call-update) | async-done | bytes 262160 | tf_op jit(solution)/shard_map/reduce_scatter | solution.py:168
  149.3 1.0 subtract_convert_fusion.2
  150.4 0.8 copy.49
  151.1 63.4 %all-to-all-done.1 = f32[8,64,2048]{2,1,0:T(8,128)} async-done(((f32[8,64,2048]{2,1,0:T(8,128)}), f32[8,64,2048]{2,1,0:T(8,128)}, u32[]{:S(2)}, u32[]{:S(2)}) %all-to-all-start.1) | async-done | bytes 4194336 | tf_op jit(solution)/shard_map/all_to_all | solution.py:202
  214.5 3.3 %reduce_sum.27 = f32[64,2048]{1,0:T(8,128)} reduce(f32[8,64,2048]{2,1,0:T(8,128)} %all-to-all-done.1, f32[]{:T(128)} %constant.62.clone.1), dimensions={0}, to_apply=%region_9.10 | reduce | flops 917504 | bytes 4718596 | tf_op jit(solution)/shard_map/reduce_sum | solution.py:209
  (72 shorter events, 3.4 us)
Async XLA Ops:
  7.2 91.6 %reduce-scatter.5.cloned.1.call-start = ((), (), s32[]{:S(2)}) async-start(), calls=%async_computation.5 | async-start | bytes 1310720 | tf_op jit(solution)/shard_map/reduce_scatter | solution.py:174
  8.7 5.7 %copy-start.12 = (f32[128,64]{0,1:T(8,128)}, f32[128,64]{0,1:T(8,128)S(1)}, u32[]{:S(2)}) copy-start(f32[128,64]{0,1:T(8,128)S(1)} %get-tuple-element.324) | copy-start | bytes 98308
  8.8 2.7 %copy-start.10 = (f32[128,64]{1,0:T(8,128)}, f32[128,64]{1,0:T(8,128)S(1)}, u32[]{:S(2)}) copy-start(f32[128,64]{1,0:T(8,128)S(1)} %copy.22) | copy-start | bytes 98308
  10.7 3.6 %copy-start.16 = (bf16[128,512]{1,0:T(8,128)(2,1)S(1)}, bf16[128,512]{1,0:T(8,128)(2,1)}, u32[]{:S(2)}) copy-start(bf16[128,512]{1,0:T(8,128)(2,1)} %param.12) | copy-start | bytes 393220
  11.5 12.3 %copy-start.18 = (u32[32]{0:T(128)S(1)}, u32[32]{0:T(128)}, u32[]{:S(2)}) copy-start(u32[32]{0:T(128)} %constant.77) | copy-start | bytes 388
  11.6 18.5 %copy-start.9 = (bf16[128,4096]{1,0:T(8,128)(2,1)S(1)}, bf16[128,4096]{1,0:T(8,128)(2,1)}, u32[]{:S(2)}) copy-start(bf16[128,4096]{1,0:T(8,128)(2,1)} %param.14) | copy-start | bytes 3145732
  12.9 18.5 %copy-start.17 = (bf16[128,512]{1,0:T(8,128)(2,1)S(1)}, bf16[128,512]{1,0:T(8,128)(2,1)}, u32[]{:S(2)}) copy-start(bf16[128,512]{1,0:T(8,128)(2,1)} %param.13) | copy-start | bytes 393220
  47.2 1.0 copy-start
  47.2 1.1 copy-start.2
  47.2 1.3 copy-start.7
  51.8 3.4 %copy-start.1 = (bf16[128,4,8,128]{3,0,2,1:T(8,128)(2,1)S(1)}, bf16[128,4,8,128]{3,0,2,1:T(8,128)(2,1)}, u32[]{:S(2)}) copy-start(bf16[128,4,8,128]{3,0,2,1:T(8,128)(2,1)} %get-tuple-element.585) | copy-start | bytes 3145732 | tf_op jit(solution)/shard_map/while
  51.8 3.4 %copy-start.8 = (bf16[512,4,128]{2,0,1:T(8,128)(2,1)S(1)}, bf16[512,4,128]{2,0,1:T(8,128)(2,1)}, u32[]{:S(2)}) copy-start(bf16[512,4,128]{2,0,1:T(8,128)(2,1)} %get-tuple-element.584) | copy-start | bytes 1572868 | tf_op jit(solution)/shard_map/while
  55.1 1.3 copy-start.3
  56.5 2.4 %copy-start.4 = (f32[512,4,128]{2,0,1:T(8,128)S(1)}, f32[512,4,128]{2,0,1:T(8,128)}, u32[]{:S(2)}) copy-start(f32[512,4,128]{2,0,1:T(8,128)} %get-tuple-element.560) | copy-start | bytes 3145732 | tf_op jit(solution)/shard_map/while
  60.3 1.0 copy-start.5
  70.3 39.6 %all-to-all-start = ((bf16[128,4,2048]{2,0,1:T(8,128)(2,1)}), bf16[128,4,2048]{2,0,1:T(8,128)(2,1)}, u32[]{:S(2)}, u32[]{:S(2)}) async-start(bf16[128,4,2048]{2,0,1:T(8,128)(2,1)} %bitcast.174), calls=%async_computation.2 | async-start | bytes 4194304 | tf_op jit(solution)/shard_map/all_to_all | solution.py:51
  99.7 15.0 %copy-start.14 = (bf16[128,512]{1,0:T(8,128)(2,1)}, bf16[128,512]{1,0:T(8,128)(2,1)S(1)}, u32[]{:S(2)}) copy-start(bf16[128,512]{1,0:T(8,128)(2,1)S(1)} %convert_element_type.49) | copy-start | bytes 393220
  114.7 6.3 %copy-start.6 = (f32[512,4,128]{2,0,1:T(8,128)S(1)}, f32[512,4,128]{2,0,1:T(8,128)}, u32[]{:S(2)}) copy-start(f32[512,4,128]{2,0,1:T(8,128)} %get-tuple-element.153) | copy-start | bytes 3145732
  114.7 7.7 %copy-start.15 = (f32[128,64]{0,1:T(8,128)S(1)}, f32[128,64]{0,1:T(8,128)}, u32[]{:S(2)}) copy-start(f32[128,64]{0,1:T(8,128)} %get-tuple-element.322) | copy-start | bytes 98308
  114.7 99.8 %all-to-all-start.1 = ((f32[8,64,2048]{2,1,0:T(8,128)}), f32[8,64,2048]{2,1,0:T(8,128)}, u32[]{:S(2)}, u32[]{:S(2)}) async-start(f32[8,64,2048]{2,1,0:T(8,128)} %fusion.48), calls=%async_computation.3 | async-start | bytes 8388608 | tf_op jit(solution)/shard_map/all_to_all | solution.py:202
  120.7 28.6 %reduce-scatter.3.cloned.1.call-start = ((), (), s32[]{:S(2)}) async-start(), calls=%async_computation.4 | async-start | bytes 1310720 | tf_op jit(solution)/shard_map/reduce_scatter | solution.py:168
  122.5 0.8 copy-start.11
  126.1 23.3 %copy-start.13 = (f32[128,64]{0,1:T(8,128)S(1)}, f32[128,64]{0,1:T(8,128)}, u32[]{:S(2)}) copy-start(f32[128,64]{0,1:T(8,128)} %copy-done.12) | copy-start | bytes 98308
Sparse Core Ops, SparseCore 0:
  67.3 31.4 reduce-scatter.4
  124.1 25.2 reduce-scatter.2
